TPU v7x, 32 devices: a whole 2x2x4 slice. The times are simulated.
32 devices in a mesh: wl: 2 (over y), row: 16 (over z, x, core).
Axes of the slice: x: 2, y: 2, z: 4, core: 2. Of those that a mesh axis runs over, the one named last changes fastest.
Arguments:
- scenes: float32 [2, 4096, 4096], P(None, 'row'), may hold values from -6 to 6
- optics: bfloat16 [4, 2, 4096, 4096], P('wl', None, 'row'), may hold values from -4 to 4
- weights: float32 [4, 2], replicated, may hold values from 0.1 to 2
Outputs:
- blurred: float32 [2, 4096, 4096], P(None, 'row', 'wl')
All inputs are finite; a program needn't handle non-finite values.
Results may differ from a plain program's by a relative error of at most 0.0003.
Values may be sent and summed in bfloat16 or wider, within the bound.
No kernel may reach another device: no remote copies, remote signals or barrier semaphores. Data moves between devices by JAX's collectives and lax.ppermute only.
A program may use at most 128 MiB of HBM per device.

v0:
```python
import math
import jax
import jax.numpy as jnp
from jax import lax
from jax.sharding import PartitionSpec as P

PRECISE = lax.Precision.HIGHEST
NARROW = 32


def phase(left_ids, right_ids, modulus, orient):
    turns = (left_ids * right_ids % modulus).astype(jnp.float32)
    angles = turns * (orient * 2.0 * math.pi / modulus)
    return (jnp.cos(angles), jnp.sin(angles))


def ids(count):
    return jnp.arange(count, dtype=jnp.int32)


def cblock(cos_part, sin_part):
    return jnp.stack([jnp.stack([cos_part, -sin_part]), jnp.stack([sin_part, cos_part])])


def small_tables(out_count, in_count, modulus, orients):
    tables = []
    for orient in orients:
        cos_part, sin_part = phase(ids(out_count)[:, None], ids(in_count)[None, :], modulus, orient)
        tables.append(cblock(cos_part, sin_part))
    return jnp.stack(tables)


def twist(values, axis_e, cos_part, sin_part):
    real = jnp.take(values, 0, axis=axis_e)
    imag = jnp.take(values, 1, axis=axis_e)
    return jnp.stack([real * cos_part - imag * sin_part, real * sin_part + imag * cos_part], axis_e)


def canon_to_groups(canon, group_count):
    mcount, span_c = (canon.shape[0], canon.shape[-1] // 2)
    mid = canon.shape[1:-1]
    if group_count == mcount:
        return canon
    span = mcount * span_c // group_count
    flat = jnp.moveaxis(canon.reshape((mcount,) + mid + (2, span_c)), 0, -2)
    flat = flat.reshape(mid + (2, group_count, span))
    return jnp.moveaxis(flat, -2, 0).reshape((group_count,) + mid + (2 * span,))


def groups_to_canon(grouped, mcount, axis_g):
    group_count = grouped.shape[axis_g]
    if group_count == mcount:
        return grouped
    moved = jnp.moveaxis(grouped, axis_g, 0)
    mid = moved.shape[1:-1]
    span = moved.shape[-1] // 2
    span_c = group_count * span // mcount
    flat = jnp.moveaxis(moved.reshape((group_count,) + mid + (2, span)), 0, -2)
    flat = flat.reshape(mid + (2, mcount, span_c))
    canon = jnp.moveaxis(flat, -2, 0).reshape((mcount,) + mid + (2 * span_c,))
    return jnp.moveaxis(canon, 0, axis_g)


def forward_rows(scenes):
    rows_here, length = (scenes.shape[1], scenes.shape[2])
    across = length // NARROW
    half_k = across // 2
    grid = scenes.reshape((2, rows_here, NARROW, across))
    first_tab = jnp.transpose(small_tables(NARROW, NARROW, NARROW, (-1.0, 1.0)), (0, 3, 1, 2, 4))
    first = jnp.einsum("oaedb,drbn->oaern", first_tab, grid, precision=PRECISE)
    tw_cos, tw_sin = ([], [])
    for orient in (-1.0, 1.0):
        cos_part, sin_part = phase(ids(NARROW)[:, None], ids(across)[None, :], length, orient)
        tw_cos.append(cos_part)
        tw_sin.append(sin_part)
    tw_cos = jnp.stack(tw_cos)[:, :, None, :]
    tw_sin = jnp.stack(tw_sin)[:, :, None, :]
    turned = twist(first, 2, tw_cos, tw_sin)
    second_tab = jnp.transpose(small_tables(half_k, across, across, (-1.0, 1.0)), (0, 2, 4, 1, 3))
    second = jnp.einsum("oaern,oenfk->oarfk", turned, second_tab, precision=PRECISE)
    signs = 1.0 - 2.0 * (ids(across) % 2).astype(jnp.float32)
    nyquist = jnp.einsum("ern,n->er", first[0, 0], signs, precision=PRECISE)
    per_block = across // NARROW
    mcount = half_k // per_block
    blocks = second.reshape((2, NARROW, rows_here, 2, mcount, per_block))
    canon = jnp.transpose(blocks, (4, 3, 2, 0, 5, 1)).reshape((mcount, 2, rows_here, 2 * across))
    canon = canon.at[0, :, :, across].set(nyquist)
    return canon


def forward_cols(columns):
    length, width = (columns.shape[1], columns.shape[2])
    across = length // NARROW
    grid = columns.reshape((2, NARROW, across, width))
    first_tab = jnp.transpose(small_tables(NARROW, NARROW, NARROW, (-1.0, 1.0)), (0, 3, 1, 2, 4))
    first = jnp.einsum("oafeb,ebnj->oafnj", first_tab, grid, precision=PRECISE)
    tw_cos, tw_sin = ([], [])
    for orient in (-1.0, 1.0):
        cos_part, sin_part = phase(ids(NARROW)[:, None], ids(across)[None, :], length, orient)
        tw_cos.append(cos_part)
        tw_sin.append(sin_part)
    tw_cos = jnp.stack(tw_cos)[:, :, :, None]
    tw_sin = jnp.stack(tw_sin)[:, :, :, None]
    turned = twist(first, 2, tw_cos, tw_sin)
    second_tab = small_tables(across, across, across, (-1.0, 1.0))
    second = jnp.einsum("ofekn,oaenj->ofkaj", second_tab, turned, precision=PRECISE)
    return second.reshape((2, 2, length, width))


def inverse_cols_half(combined, group_count, half_index, part=0, parts=1):
    length, width = (combined.shape[1], combined.shape[2])
    across = length // NARROW
    grid = combined.reshape((2, NARROW, across, width))
    first_tab = jnp.transpose(small_tables(NARROW, NARROW, NARROW, (1.0,))[0], (2, 0, 1, 3))
    first = jnp.einsum("afeb,ebnj->afnj", first_tab, grid, precision=PRECISE)
    cos_part, sin_part = phase(ids(NARROW)[:, None], ids(across)[None, :], length, 1.0)
    turned = twist(first, 1, cos_part[:, :, None], sin_part[:, :, None])
    per_group = across // group_count
    per_half = per_group // 2
    per_part = per_half // parts
    k_ids = ids(per_part)[None, :] + part * per_part
    k_ids = ids(group_count)[:, None] * per_group + half_index * per_half + k_ids
    cos_k, sin_k = phase(k_ids.reshape((-1, 1)), ids(across)[None, :], across, 1.0)
    second_tab = jnp.transpose(cblock(cos_k, sin_k), (0, 2, 1, 3))
    second = jnp.einsum("fken,aenj->fkaj", second_tab, turned, precision=PRECISE)
    return second.reshape((2, group_count, per_part * NARROW, width))


def inverse_cols(combined):
    length, width = (combined.shape[1], combined.shape[2])
    across = length // NARROW
    grid = combined.reshape((2, NARROW, across, width))
    first_tab = jnp.transpose(small_tables(NARROW, NARROW, NARROW, (1.0,))[0], (2, 0, 1, 3))
    first = jnp.einsum("afeb,ebnj->afnj", first_tab, grid, precision=PRECISE)
    cos_part, sin_part = phase(ids(NARROW)[:, None], ids(across)[None, :], length, 1.0)
    turned = twist(first, 1, cos_part[:, :, None], sin_part[:, :, None])
    second_tab = jnp.transpose(small_tables(across, across, across, (1.0,))[0], (0, 2, 1, 3))
    second = jnp.einsum("fken,aenj->fkaj", second_tab, turned, precision=PRECISE)
    return second.reshape((2, length, width))


def inverse_rows(canon, length, scale, k_count=None, k_start=0):
    mcount, rows_here, width = (canon.shape[1], canon.shape[2], canon.shape[3])
    across = width // 2
    k_count = across if k_count is None else k_count
    first_tab = jnp.transpose(small_tables(NARROW, mcount, NARROW, (1.0, -1.0)), (0, 3, 1, 2, 4))
    first = jnp.einsum("oafem,emRj->oafRj", first_tab, canon, precision=PRECISE)
    lower = first[0, :, :, :, :across]
    upper = first[1, :, :, :, across:]
    flip_gain = -2.0 * (ids(NARROW) % 2).astype(jnp.float32)
    fix = flip_gain[:, None, None] * canon[:, 0, :, across][None]
    lane0 = (ids(across) == 0)[None, None, None, :]
    upper = jnp.where(lane0, upper + fix[..., None], upper)
    cos_up, sin_up = phase(ids(NARROW)[:, None], ids(across)[None, :], length, 1.0)
    cos_dn, sin_dn = phase(ids(NARROW)[:, None], ids(across)[None, :], length, -1.0)
    lower = twist(lower, 1, cos_up[:, None, :], sin_up[:, None, :])
    upper = twist(upper, 1, cos_dn[:, None, :], sin_dn[:, None, :])
    tabs = []
    for orient in (1.0, -1.0):
        k_ids = ids(k_count)[:, None] + k_start
        cos_part, sin_part = phase(k_ids, ids(across)[None, :], across, orient)
        tabs.append(cblock(cos_part, sin_part))
    tabs = jnp.transpose(jnp.stack(tabs) * scale, (0, 2, 4, 1, 3))
    out = jnp.einsum("aeRu,eufk->aRfk", lower, tabs[0], precision=PRECISE)
    out = out + jnp.einsum("aeRu,eufk->aRfk", upper, tabs[1], precision=PRECISE)
    return jnp.transpose(out, (2, 1, 3, 0)).reshape((2, rows_here, k_count * NARROW))


def pair_optics(optics):
    length = optics.shape[-1]
    across = length // NARROW
    half = length // 2
    mcount = half // across
    block = [lax.slice_in_dim(optics, across * i, across * (i + 1), axis=3) for i in range(NARROW)]
    windows = []
    for m in range(mcount):
        second = block[half // across if m == 0 else NARROW - m]
        windows.append(jnp.concatenate([block[NARROW - 1 - m], second], -1))
    windows = jnp.stack(windows)
    src = ids(2 * across)[:, None]
    dst = ids(across)[None, :]
    picker = jnp.logical_or(
        jnp.logical_and(src == across - dst, dst > 0), jnp.logical_and(src == across, dst == 0)
    ).astype(optics.dtype)
    mirrored = jnp.einsum("mwcpv,vu->mwcpu", windows, picker, preferred_element_type=jnp.float32)
    lower = jnp.stack(block[:mcount])
    return jnp.concatenate([lower, mirrored.astype(optics.dtype)], -1)


def local(scenes, optics, weights):
    row_count = lax.axis_size("row")
    length = scenes.shape[2]
    across = length // NARROW
    norm_factor = 1.0 / (float(length) * float(length))
    wl_index = lax.axis_index("wl")
    local_waves = optics.shape[0]
    weight_rows = lax.dynamic_slice_in_dim(weights, wl_index * local_waves, local_waves, 0)
    first_row = lax.axis_index("row") == 0
    wl_count = lax.axis_size("wl")
    rows_here = scenes.shape[1]
    own_rows = rows_here // wl_count
    if wl_count == 2 and own_rows * wl_count == rows_here:
        mine = lax.dynamic_slice_in_dim(scenes, wl_index * own_rows, own_rows, 1)
        canon = forward_rows(mine)
        mcount = canon.shape[0]
        sent = canon_to_groups(canon, row_count)
        got = lax.all_to_all(sent, "row", split_axis=0, concat_axis=2, tiled=True)[0]
        other = lax.ppermute(got, "wl", perm=[(0, 1), (1, 0)])
        got = got.reshape((2, row_count, own_rows, got.shape[-1]))
        other = other.reshape(got.shape)
        first_half = jnp.where(wl_index == 0, got, other)
        second_half = jnp.where(wl_index == 0, other, got)
        got = jnp.stack([first_half, second_half], 2).reshape((2, length, got.shape[-1]))
    else:
        canon = forward_rows(scenes)
        mcount = canon.shape[0]
        sent = canon_to_groups(canon, row_count)
        got = lax.all_to_all(sent, "row", split_axis=0, concat_axis=2, tiled=True)[0]
    spec = forward_cols(got)
    optic_canon = pair_optics(optics)
    optic_sent = canon_to_groups(optic_canon, row_count)
    optic_got = lax.all_to_all(optic_sent, "row", split_axis=0, concat_axis=3, tiled=True)[0]
    width = spec.shape[-1]
    span = width // 2
    lane_ids = ids(width)
    itself = jnp.logical_and(first_row, lane_ids % span == 0)
    direct = spec[0]
    flipped = spec[1]
    swapped = jnp.concatenate([flipped[..., span:], flipped[..., :span]], -1)
    partner = jnp.where(itself, flipped, swapped)
    mirror_real = partner[0]
    mirror_imag = -partner[1]
    even_real = 0.5 * (direct[0] + mirror_real)
    even_imag = 0.5 * (direct[1] + mirror_imag)
    odd_real = 0.5 * (direct[0] - mirror_real)
    odd_imag = 0.5 * (direct[1] - mirror_imag)
    combined_real = jnp.zeros_like(even_real)
    combined_imag = jnp.zeros_like(even_imag)
    for colour in range(local_waves):
        mixed_real = weight_rows[colour, 0] * even_real + weight_rows[colour, 1] * odd_real
        mixed_imag = weight_rows[colour, 0] * even_imag + weight_rows[colour, 1] * odd_imag
        resp_real = optic_got[colour, 0].astype(jnp.float32)
        resp_imag = optic_got[colour, 1].astype(jnp.float32)
        combined_real = combined_real + resp_real * mixed_real - resp_imag * mixed_imag
        combined_imag = combined_imag + resp_real * mixed_imag + resp_imag * mixed_real
    stacked = jnp.stack([combined_real, combined_imag])
    back = inverse_cols(stacked)
    if wl_count != 2 or own_rows * wl_count != rows_here:
        back = back.reshape((2, row_count, rows_here, width))
        returned = lax.all_to_all(back, "row", split_axis=1, concat_axis=1, tiled=True)
        returned = groups_to_canon(returned, mcount, 1)
        result_image = inverse_rows(returned, length, norm_factor)
        return lax.psum_scatter(result_image, "wl", scatter_dimension=2, tiled=True)
    per_group = across // row_count
    if per_group % 2 == 0 and per_group * row_count == across:
        parts = 4 if per_group % 8 == 0 else 1
        incoming = []
        for part in range(parts):
            given = inverse_cols_half(stacked, row_count, 1 - wl_index, part, parts)
            incoming.append(lax.ppermute(given, "wl", perm=[(0, 1), (1, 0)]))
        incoming = jnp.concatenate(incoming, 2)
        kept = inverse_cols_half(stacked, row_count, wl_index)
    else:
        back = back.reshape((2, row_count, 2, own_rows, width))
        kept = lax.dynamic_index_in_dim(back, wl_index, 2, keepdims=False)
        given = lax.dynamic_index_in_dim(back, 1 - wl_index, 2, keepdims=False)
        incoming = lax.ppermute(given, "wl", perm=[(0, 1), (1, 0)])
    summed = kept + incoming
    returned = lax.all_to_all(summed, "row", split_axis=1, concat_axis=1, tiled=True)
    returned = groups_to_canon(returned, mcount, 1)
    k_half = across // 2
    theirs = inverse_rows(returned, length, norm_factor, k_half, (1 - wl_index) * k_half)
    taken = lax.ppermute(theirs, "wl", perm=[(0, 1), (1, 0)])
    mine = inverse_rows(returned, length, norm_factor, k_half, wl_index * k_half)
    upper = jnp.where(wl_index == 0, mine, taken)
    lower = jnp.where(wl_index == 0, taken, mine)
    return jnp.concatenate([upper, lower], 1)


def solution(mesh):
    in_specs = (P(None, "row", None), P("wl", None, "row", None), P())
    out_specs = P(None, "row", "wl")
    return jax.shard_map(local, mesh=mesh, in_specs=in_specs, out_specs=out_specs, check_vma=False)
```

profile of v0, /device:TPU:10, one launch (start us, length us, event | category | flops | bytes accessed | tf_op | source)
XLA Modules:
  0.0 713.1 jit_solution(16438513354789603543)
XLA Ops:
  5.1 6.8 fusion.46
  15.1 13.9 %fusion.17 = f32[2,32,128,2,64,1]{2,4,5,3,1,0:T(8,128)S(1)} fusion(f32[2,32,2,128,128,1]{4,1,3,0,2,5:T(8,128)S(1)} %maximum_bitcast_fusion.1, f32[1,2,2,64,128]{4,3,2,1,0:T(8,128)S(1)} %maximum_bitcast_fusion.22, f32[1,2,2,64,128]{4,3,2,1,0:T(8,128)S(1)} %maximum_bitcast_fusion.21), kind=kOutput, calls=%fused_computation.26 | convolution fusion | flops 3221291008 | bytes 12845056 | tf_op jit(solution)/shard_map/oaern,oenfk->oarfk/dot_general | solution.py:80
  39.4 6.2 all-to-all-start.1
  98.0 7.8 %pad_maximum_fusion = bf16[16,2,2,256,256]{3,4,2,1,0:T(8,128)(2,1)} fusion(bf16[16,2,2,256,128]{3,4,2,1,0:T(8,128)(2,1)} %convolution_convert_fusion, bf16[16,2,2,256,128]{3,4,2,1,0:T(8,128)(2,1)} %bitcast_dynamic-update-slice_fusion.15), kind=kLoop, calls=%fused_computation.5 | loop fusion | flops 16777216 | bytes 16777216 | tf_op jit(solution)/shard_map/concatenate | solution.py:187
  105.9 32.1 %all-to-all-done.1 = f32[16,2,128,256]{2,3,1,0:T(8,128)} async-done(((f32[16,2,128,256]{2,3,1,0:T(8,128)}), f32[16,2,128,256]{2,3,1,0:T(8,128)}, u32[]{:S(2)}, u32[]{:S(2)}) %all-to-all-start.1) | async-done | bytes 4194336 | tf_op jit(solution)/shard_map/all_to_all | solution.py:207
  160.9 80.8 %collective-permute-done = f32[2,2048,256]{2,1,0:T(8,128)} collective-permute-done((f32[2,2048,256]{2,1,0:T(8,128)}, f32[2,2048,256]{2,1,0:T(8,128)}, u32[]{:S(2)}, u32[]{:S(2)}) %collective-permute-start) | collective-permute-done | bytes 4194336 | tf_op jit(solution)/shard_map/ppermute | solution.py:208
  255.0 13.3 %copy.175 = f32[2,16,2,128,256]{4,2,1,0,3:T(2,128)} copy(f32[2,16,2,128,256]{3,4,0,1,2:T(8,128)} %pad_maximum_fusion.1) | data formatting | bytes 16777216 | tf_op jit(solution)/shard_map/stack | solution.py:213
  268.3 10.9 %reshape.2175 = f32[2,32,128,256,1,1]{3,1,0,2,4,5:T(8,128)} reshape(f32[2,16,2,128,256]{4,2,1,0,3:T(2,128)} %copy.175) | data formatting | bytes 16777216 | tf_op jit(solution)/shard_map/reshape;reshape | solution.py:94
  279.2 16.7 %fusion.19 = f32[2,32,2,128,256]{4,1,3,2,0:T(8,128)S(1)} fusion(f32[2,32,128,256,1,1]{3,1,0,2,4,5:T(8,128)} %reshape.2175, f32[1,2,2,32,32]{4,3,2,1,0:T(8,128)S(1)} %fusion.98, f32[1,2,2,32,32]{4,3,2,1,0:T(8,128)S(1)} %maximum_bitcast_fusion.31), kind=kOutput, calls=%fused_computation.30 | convolution fusion | flops 3221233664 | bytes 25198592 | tf_op jit(solution)/shard_map/oafeb,ebnj->oafnj/dot_general | solution.py:96
  295.9 6.0 subtract_bitcast_fusion
  306.9 25.0 %fusion.22 = f32[2,2,128,32,256]{4,2,3,1,0:T(8,128)S(1)} fusion(f32[2,32,2,128,256,1]{4,1,3,0,2,5:T(8,128)S(1)} %maximum_bitcast_fusion, f32[1,2,2,128,128]{4,3,2,1,0:T(8,128)} %maximum_bitcast_fusion.12, f32[1,2,2,128,128]{4,3,2,1,0:T(8,128)} %maximum_bitcast_fusion.11), kind=kOutput, calls=%fused_computation.31 | convolution fusion | flops 12885032960 | bytes 34078720 | tf_op jit(solution)/shard_map/ofekn,oaenj->ofkaj/dot_general | solution.py:106
  331.9 5.8 copy-done.3
  342.1 8.2 %copy.181 = f32[1,2,128,32,256]{4,3,2,1,0:T(8,128)S(1)} copy(f32[1,2,128,32,256]{4,2,3,1,0:T(8,128)} %slice.369) | data formatting | bytes 16777216 | tf_op jit(solution)/shard_map/slice | solution.py:228
  367.5 11.5 %copy.166 = bf16[1,2,2,16,256,256]{5,4,3,2,1,0:T(8,128)(2,1)} copy(bf16[1,2,2,16,256,256]{4,5,2,1,3,0:T(8,128)(2,1)} %bitcast.54) | data formatting | bytes 16777216 | tf_op jit(solution)/shard_map/all_to_all | solution.py:222
  379.0 11.1 %fusion.32 = (f32[1,4096,256]{2,1,0:T(8,128)S(1)}, f32[1,4096,256]{2,1,0:T(8,128)S(1)}) fusion(bf16[2,2,4096,256]{3,2,1,0:T(8,128)(2,1)} %bitcast.577, f32[]{:T(128)} %bitcast.125, f32[]{:T(128)} %bitcast.124, f32[2,4096,256]{2,1,0:T(8,128)} %maximum_select_fusion, f32[1,1,128,32,256]{4,3,2,1,0:T(8,128)} %copy.180, f32[]{:T(128)} %bitcast.130, f32[]{:T(128)} %bitcast.129, ...), kind=kLoop, calls=%fused_computation.49 | loop fusion | flops 36700160 | bytes 33554448 | tf_op jit(solution)/shard_map/sub | solution.py:244
  395.0 7.7 %fusion.47 = f32[32,2,128,256]{3,0,2,1:T(8,128)S(1)} fusion(f32[1,32,128,256]{3,1,0,2:T(8,128)S(1)} %copy.184, f32[1,32,128,256]{3,1,0,2:T(8,128)S(1)} %copy.183, f32[1,2,32,32]{3,2,1,0:T(8,128)S(1)} %copy-done.17, f32[1,2,32,32]{3,2,1,0:T(8,128)S(1)} %copy-done.15), kind=kOutput, calls=%fused_computation.90 | convolution fusion | flops 1612713984 | bytes 16793600 | tf_op jit(solution)/shard_map/afeb,ebnj->afnj/dot_general | solution.py:115
  405.9 9.4 %fusion.57 = f32[2,16,32,256]{3,1,2,0:T(8,128)S(1)} fusion(f32[32,2,128,256]{3,0,2,1:T(8,128)S(1)} %pad_maximum_fusion.2, f32[1,2,16,128]{3,2,1,0:T(8,128)S(1)} %copy-done.25, f32[1,2,16,128]{3,2,1,0:T(8,128)S(1)} %copy-done.24), kind=kOutput, calls=%fused_computation.111 | convolution fusion | flops 805314560 | bytes 9469952 | tf_op jit(solution)/shard_map/fken,aenj->fkaj/dot_general | solution.py:125
  416.8 10.7 %fusion.60 = f32[2,16,32,256]{3,1,2,0:T(8,128)} fusion(f32[32,2,128,256]{3,0,2,1:T(8,128)S(1)} %pad_maximum_fusion.2, f32[1,2,16,128]{3,2,1,0:T(8,128)S(1)} %copy-done.27, f32[1,2,16,128]{3,2,1,0:T(8,128)S(1)} %copy-done.26), kind=kOutput, calls=%fused_computation.112 | convolution fusion | flops 805314560 | bytes 9469952 | tf_op jit(solution)/shard_map/fken,aenj->fkaj/dot_general | solution.py:125
  428.1 10.5 %fusion.63 = f32[2,16,32,256]{3,1,2,0:T(8,128)} fusion(f32[32,2,128,256]{3,0,2,1:T(8,128)S(1)} %pad_maximum_fusion.2, f32[1,2,16,128]{3,2,1,0:T(8,128)S(1)} %copy-done.29, f32[1,2,16,128]{3,2,1,0:T(8,128)S(1)} %copy-done.28), kind=kOutput, calls=%fused_computation.113 | convolution fusion | flops 805314560 | bytes 9469952 | tf_op jit(solution)/shard_map/fken,aenj->fkaj/dot_general | solution.py:125
  440.1 10.5 %fusion.66 = f32[2,16,32,256]{3,1,2,0:T(8,128)} fusion(f32[32,2,128,256]{3,0,2,1:T(8,128)S(1)} %pad_maximum_fusion.2, f32[1,2,16,128]{3,2,1,0:T(8,128)S(1)} %copy-done.31, f32[1,2,16,128]{3,2,1,0:T(8,128)S(1)} %copy-done.30), kind=kOutput, calls=%fused_computation.114 | convolution fusion | flops 805314560 | bytes 9469952 | tf_op jit(solution)/shard_map/fken,aenj->fkaj/dot_general | solution.py:125
  451.6 13.0 %fusion.48 = f32[2,64,32,256]{3,1,2,0:T(8,128)S(1)} fusion(f32[32,2,128,256]{3,0,2,1:T(8,128)} %copy-done.2, f32[1,2,64,128]{3,2,1,0:T(8,128)S(1)} %get-tuple-element.164, f32[1,2,64,128]{3,2,1,0:T(8,128)S(1)} %get-tuple-element.163), kind=kOutput, calls=%fused_computation.92 | convolution fusion | flops 3221258240 | bytes 12713984 | tf_op jit(solution)/shard_map/fken,aenj->fkaj/dot_general | solution.py:125
  467.1 19.4 %collective-permute-done.3 = f32[2,16,32,256]{3,1,2,0:T(8,128)} collective-permute-done((f32[2,16,32,256]{3,1,2,0:T(8,128)}, f32[2,16,32,256]{3,1,2,0:T(8,128)}, u32[]{:S(2)}, u32[]{:S(2)}) %collective-permute-start.3) | collective-permute-done | bytes 1048608 | tf_op jit(solution)/shard_map/ppermute | solution.py:260
  486.5 20.7 %collective-permute-done.4 = f32[2,16,32,256]{3,1,2,0:T(8,128)} collective-permute-done((f32[2,16,32,256]{3,1,2,0:T(8,128)}, f32[2,16,32,256]{3,1,2,0:T(8,128)}, u32[]{:S(2)}, u32[]{:S(2)}) %collective-permute-start.4) | collective-permute-done | bytes 1048608 | tf_op jit(solution)/shard_map/ppermute | solution.py:260
  507.2 6.0 maximum_add_fusion
  517.7 6.0 all-to-all-start.2
  524.6 91.5 %all-to-all-done.2 = f32[2,16,128,256]{3,2,0,1:T(8,128)} async-done(((f32[2,16,128,256]{3,2,0,1:T(8,128)}), f32[2,16,128,256]{3,2,0,1:T(8,128)}, u32[]{:S(2)}, u32[]{:S(2)}) %all-to-all-start.2) | async-done | bytes 4194336 | tf_op jit(solution)/shard_map/all_to_all | solution.py:269
  616.0 18.1 %convolution_bitcast_fusion = f32[2,32,2,128,256]{4,1,3,2,0:T(8,128)S(1)} fusion(f32[2,16,128,256,1,1]{3,2,0,1,5,4:T(8,128)} %bitcast.181, f32[1,2,2,32,16]{3,4,2,1,0:T(8,128)S(1)} %maximum_bitcast_fusion.45, f32[1,2,2,32,16]{3,4,2,1,0:T(8,128)S(1)} %maximum_bitcast_fusion.44), kind=kOutput, calls=%fused_computation.32 | convolution fusion | flops 1610616832 | bytes 20987904 | tf_op jit(solution)/shard_map/oafem,emRj->oafRj/dot_general | solution.py:147
  639.9 6.9 fusion.38
  646.8 7.1 fusion.51
  657.2 8.1 %fusion.40 = f32[32,128,2,64,1]{1,3,4,2,0:T(8,128)S(1)} fusion(f32[32,2,128,128,1]{3,0,2,1,4:T(8,128)} %copy-done.6, f32[2,2,128,2,64]{2,4,1,3,0:T(8,128)S(1)} %fusion.75), kind=kOutput, calls=%fused_computation.83 | convolution fusion | flops 1610612736 | bytes 6422528 | tf_op jit(solution)/shard_map/aeRu,eufk->aRfk/dot_general | solution.py:165
  665.3 6.9 fusion.52
  673.4 29.8 %collective-permute-done.5 = f32[2,128,2048]{1,2,0:T(8,128)} collective-permute-done((f32[2,128,2048]{1,2,0:T(8,128)S(1)}, f32[2,128,2048]{1,2,0:T(8,128)}, u32[]{:S(2)}, u32[]{:S(2)}) %collective-permute-start.5) | collective-permute-done | bytes 2097184 | tf_op jit(solution)/shard_map/ppermute | solution.py:273
  (248 shorter events, 170.6 us)
Async XLA Ops:
  0.0 150.5 %copy-start = (f32[4,2]{0,1:T(2,128)S(1)}, f32[4,2]{0,1:T(2,128)}, u32[]{:S(2)}) copy-start(f32[4,2]{0,1:T(2,128)} %param.23) | copy-start | bytes 100
  29.0 3.5 copy-start.35
  39.4 98.6 %all-to-all-start.1 = ((f32[16,2,128,256]{2,3,1,0:T(8,128)}), f32[16,2,128,256]{2,3,1,0:T(8,128)}, u32[]{:S(2)}, u32[]{:S(2)}) async-start(f32[16,2,128,256]{2,3,1,0:T(8,128)} %scatter.4), calls=%async_computation.1 | async-start | bytes 8388608 | tf_op jit(solution)/shard_map/all_to_all | solution.py:207
  45.7 47.5 %copy-start.32 = (pred[128]{0:T(512)(128)(4,1)}, pred[128]{0:T(512)(128)(4,1)S(1)}, u32[]{:S(2)}) copy-start(pred[128]{0:T(512)(128)(4,1)S(1)} %get-tuple-element.218) | copy-start | bytes 388
  57.3 8.8 %copy-start.8 = (bf16[2,2,256,128]{3,2,1,0:T(8,128)(2,1)S(1)}, bf16[2,2,256,128]{3,2,1,0:T(8,128)(2,1)}, u32[]{:S(2)}) copy-start(bf16[2,2,256,128]{3,2,1,0:T(8,128)(2,1)} %get-tuple-element.143) | copy-start | bytes 786436
  84.5 8.7 %copy-start.34 = (s32[128]{0:T(128)S(1)}, s32[128]{0:T(128)}, u32[]{:S(2)}) copy-start(s32[128]{0:T(128)} %iota_subtract_fusion) | copy-start | bytes 1540
  138.0 229.5 %all-to-all-start = ((bf16[16,2,2,256,256]{3,4,2,1,0:T(8,128)(2,1)}), bf16[16,2,2,256,256]{3,4,2,1,0:T(8,128)(2,1)}, u32[]{:S(2)}, u32[]{:S(2)}) async-start(bf16[16,2,2,256,256]{3,4,2,1,0:T(8,128)(2,1)} %pad_maximum_fusion), calls=%async_computation | async-start | bytes 16777216 | tf_op jit(solution)/shard_map/all_to_all | solution.py:222
  143.4 6.9 copy-start.13
  143.4 7.0 copy-start.11
  148.7 92.9 %collective-permute-start = (f32[2,2048,256]{2,1,0:T(8,128)}, f32[2,2048,256]{2,1,0:T(8,128)}, u32[]{:S(2)}, u32[]{:S(2)}) collective-permute-start(f32[2,2048,256]{2,1,0:T(8,128)} %bitcast.586), channel_id=1, source_target_pairs={{0,16},{16,0},{1,17},{17,1},{2,18},{18,2},{3,19},{19,3},{4,20},{20... | collective-permute-start | bytes 12582920 | tf_op jit(solution)/shard_map/ppermute | solution.py:208
  153.8 5.6 copy-start.20
  153.8 5.6 copy-start.22
  331.9 5.8 copy-start.3
  395.0 7.7 %copy-start.18 = (f32[32,128]{0,1:T(8,128)S(1)}, f32[32,128]{0,1:T(8,128)}, u32[]{:S(2)}) copy-start(f32[32,128]{0,1:T(8,128)} %copy.185) | copy-start | bytes 49156
  395.0 7.7 %copy-start.19 = (f32[32,128]{0,1:T(8,128)S(1)}, f32[32,128]{0,1:T(8,128)}, u32[]{:S(2)}) copy-start(f32[32,128]{0,1:T(8,128)} %copy.186) | copy-start | bytes 49156
  405.8 34.3 %copy-start.2 = (f32[32,2,128,256]{3,0,2,1:T(8,128)}, f32[32,2,128,256]{3,0,2,1:T(8,128)S(1)}, u32[]{:S(2)}) copy-start(f32[32,2,128,256]{3,0,2,1:T(8,128)S(1)} %pad_maximum_fusion.2) | copy-start | bytes 25165828
  405.9 11.0 %copy-start.26 = (f32[1,2,16,128]{3,2,1,0:T(8,128)S(1)}, f32[1,2,16,128]{3,2,1,0:T(8,128)}, u32[]{:S(2)}) copy-start(f32[1,2,16,128]{3,2,1,0:T(8,128)} %get-tuple-element.179) | copy-start | bytes 49156
  405.9 11.0 %copy-start.27 = (f32[1,2,16,128]{3,2,1,0:T(8,128)S(1)}, f32[1,2,16,128]{3,2,1,0:T(8,128)}, u32[]{:S(2)}) copy-start(f32[1,2,16,128]{3,2,1,0:T(8,128)} %get-tuple-element.180) | copy-start | bytes 49156
  415.2 51.8 %collective-permute-start.1 = (f32[2,16,32,256]{3,1,2,0:T(8,128)S(1)}, f32[2,16,32,256]{3,1,2,0:T(8,128)S(1)}, u32[]{:S(2)}, u32[]{:S(2)}) collective-permute-start(f32[2,16,32,256]{3,1,2,0:T(8,128)S(1)} %fusion.57), channel_id=1, source_target_pairs={{0,16},{16,0},{1,17},{17,1},{2,18},{18,2},{3,19},{19,3},{4,20},{20... | collective-permute-start | bytes 3145736 | tf_op jit(solution)/shard_map/ppermute | solution.py:260
  416.8 11.3 %copy-start.28 = (f32[1,2,16,128]{3,2,1,0:T(8,128)S(1)}, f32[1,2,16,128]{3,2,1,0:T(8,128)}, u32[]{:S(2)}) copy-start(f32[1,2,16,128]{3,2,1,0:T(8,128)} %get-tuple-element.181) | copy-start | bytes 49156
  416.8 11.3 %copy-start.29 = (f32[1,2,16,128]{3,2,1,0:T(8,128)S(1)}, f32[1,2,16,128]{3,2,1,0:T(8,128)}, u32[]{:S(2)}) copy-start(f32[1,2,16,128]{3,2,1,0:T(8,128)} %get-tuple-element.182) | copy-start | bytes 49156
  427.6 39.5 %collective-permute-start.2 = (f32[2,16,32,256]{3,1,2,0:T(8,128)}, f32[2,16,32,256]{3,1,2,0:T(8,128)S(1)}, u32[]{:S(2)}, u32[]{:S(2)}) collective-permute-start(f32[2,16,32,256]{3,1,2,0:T(8,128)} %fusion.60), channel_id=1, source_target_pairs={{0,16},{16,0},{1,17},{17,1},{2,18},{18,2},{3,19},{19,3},{4,20},{20... | collective-permute-start | bytes 3145736 | tf_op jit(solution)/shard_map/ppermute | solution.py:260
  428.1 12.0 %copy-start.30 = (f32[1,2,16,128]{3,2,1,0:T(8,128)S(1)}, f32[1,2,16,128]{3,2,1,0:T(8,128)}, u32[]{:S(2)}) copy-start(f32[1,2,16,128]{3,2,1,0:T(8,128)} %get-tuple-element.183) | copy-start | bytes 49156
  428.1 12.0 %copy-start.31 = (f32[1,2,16,128]{3,2,1,0:T(8,128)S(1)}, f32[1,2,16,128]{3,2,1,0:T(8,128)}, u32[]{:S(2)}) copy-start(f32[1,2,16,128]{3,2,1,0:T(8,128)} %get-tuple-element.184) | copy-start | bytes 49156
  438.6 47.9 %collective-permute-start.3 = (f32[2,16,32,256]{3,1,2,0:T(8,128)}, f32[2,16,32,256]{3,1,2,0:T(8,128)}, u32[]{:S(2)}, u32[]{:S(2)}) collective-permute-start(f32[2,16,32,256]{3,1,2,0:T(8,128)} %fusion.63), channel_id=1, source_target_pairs={{0,16},{16,0},{1,17},{17,1},{2,18},{18,2},{3,19},{19,3},{4,20},{20... | collective-permute-start | bytes 3145736 | tf_op jit(solution)/shard_map/ppermute | solution.py:260
  450.6 56.6 %collective-permute-start.4 = (f32[2,16,32,256]{3,1,2,0:T(8,128)}, f32[2,16,32,256]{3,1,2,0:T(8,128)}, u32[]{:S(2)}, u32[]{:S(2)}) collective-permute-start(f32[2,16,32,256]{3,1,2,0:T(8,128)} %fusion.66), channel_id=1, source_target_pairs={{0,16},{16,0},{1,17},{17,1},{2,18},{18,2},{3,19},{19,3},{4,20},{20... | collective-permute-start | bytes 3145736 | tf_op jit(solution)/shard_map/ppermute | solution.py:260
  517.7 98.3 %all-to-all-start.2 = ((f32[2,16,128,256]{3,2,0,1:T(8,128)}), f32[2,16,128,256]{3,2,0,1:T(8,128)}, u32[]{:S(2)}, u32[]{:S(2)}) async-start(f32[2,16,128,256]{3,2,0,1:T(8,128)} %copy.194), calls=%async_computation.2 | async-start | bytes 8388608 | tf_op jit(solution)/shard_map/all_to_all | solution.py:269
  638.8 8.1 %copy-start.4 = (f32[32,2,128,128,1]{3,0,2,1,4:T(8,128)}, f32[32,2,128,128,1]{3,0,2,1,4:T(8,128)S(1)}, u32[]{:S(2)}) copy-start(f32[32,2,128,128,1]{3,0,2,1,4:T(8,128)S(1)} %maximum_bitcast_fusion.4) | copy-start | bytes 12582916
  639.9 14.0 %copy-start.6 = (f32[32,2,128,128,1]{3,0,2,1,4:T(8,128)}, f32[32,2,128,128,1]{3,0,2,1,4:T(8,128)S(1)}, u32[]{:S(2)}) copy-start(f32[32,2,128,128,1]{3,0,2,1,4:T(8,128)S(1)} %maximum_bitcast_fusion.5) | copy-start | bytes 12582916
  655.2 48.0 %collective-permute-start.5 = (f32[2,128,2048]{1,2,0:T(8,128)S(1)}, f32[2,128,2048]{1,2,0:T(8,128)}, u32[]{:S(2)}, u32[]{:S(2)}) collective-permute-start(f32[2,128,2048]{1,2,0:T(8,128)S(1)} %bitcast.587), channel_id=1, source_target_pairs={{0,16},{16,0},{1,17},{17,1},{2,18},{18,2},{3,19},{19,3},{4,20},{20... | collective-permute-start | bytes 6291464 | tf_op jit(solution)/shard_map/ppermute | solution.py:273
  656.8 8.5 %copy-start.5 = (f32[32,2,128,128,1]{3,0,2,1,4:T(8,128)S(1)}, f32[32,2,128,128,1]{3,0,2,1,4:T(8,128)}, u32[]{:S(2)}) copy-start(f32[32,2,128,128,1]{3,0,2,1,4:T(8,128)} %copy-done.4) | copy-start | bytes 12582916
  705.1 7.7 %copy-start.1 = (f32[4,2]{0,1:T(2,128)S(1)}, f32[4,2]{0,1:T(2,128)}, u32[]{:S(2)}) copy-start(f32[4,2]{0,1:T(2,128)} %param.23) | copy-start | bytes 100
  (13 other events, 21.9 us)
where the time goes:
time: 724 us; the launch traced here: 713 us
  waiting for transfers between devices  274 us (38%)
  matrix products  178 us (25%)
  local copies, waits for them, and re-layouts  159 us (22%)
  other arithmetic  72.8 us (10%)
  starting transfers between devices  24.9 us (3%)
    all_to_all x1, waiting for transfers between devices, local(): lax.all_to_all(summed, 'row', split_axis=1, concat_axis=1, tiled=True)  91.5 us
    ppermute x1, waiting for transfers between devices, local(): other = lax.ppermute(got, 'wl', perm=[(0, 1), (1, 0)])  80.8 us
    dot_general x5, matrix products, inverse_cols_half(): jnp.einsum('fken,aenj->fkaj', second_tab, turned, precision=PRECISE)  54.1 us
    unnamed x118, local copies, waits for them, and re-layouts  48.7 us
    ppermute x4, waiting for transfers between devices, local(): incoming.append(lax.ppermute(given, 'wl', perm=[(0, 1), (1, 0)]))  40.1 us
    all_to_all x1, waiting for transfers between devices, local(): lax.all_to_all(sent, 'row', split_axis=0, concat_axis=2, tiled=True)[0]  32.1 us
    ppermute x1, waiting for transfers between devices, local(): taken = lax.ppermute(theirs, 'wl', perm=[(0, 1), (1, 0)])  29.8 us
    dot_general x1, matrix products, forward_cols(): jnp.einsum('ofekn,oaenj->ofkaj', second_tab, turned, precision=PRECISE)  25 us
  transfers between devices with their start and end apart: 9, of which 6 were waited for; matrix products, arithmetic and copies ran while one was open for 36% of the time, Pallas kernels for 0%

commit v1 on v0

--- a/solution.py
+++ b/solution.py
@@ -1,3 +1,4 @@
+import functools
 import math
 import jax
 import jax.numpy as jnp
@@ -6,6 +7,42 @@
 
 PRECISE = lax.Precision.HIGHEST
 NARROW = 32
+
+
+def rest_bars(sample, where_dim, arr):
+    a_now = sample.shape
+    arr_next = sample.reshape(
+        *a_now[:where_dim], arr, a_now[where_dim] // arr, *a_now[where_dim + 1 :]
+    )
+    local_part = jnp.moveaxis(arr_next, where_dim, 0)
+    return local_part
+
+
+def find_object(frame_in, axis_k):
+    frame_in = jnp.moveaxis(frame_in, 0, axis_k)
+    even = frame_in.shape
+    before = frame_in.reshape(*even[:axis_k], even[axis_k] * even[axis_k + 1], *even[axis_k + 2 :])
+    return before
+
+
+def _settle_things(obj, row_axis, vector, local_block):
+    h_now = jax.lax.psum(1, row_axis)
+    local_out = jax.lax.axis_index(row_axis)
+    current_arr, piece_next = (h_now, local_out)
+    row_out = rest_bars(obj, vector, current_arr)
+    xs_all = [row_out[piece_next]]
+    for dd in range(1, current_arr):
+        local_now = row_out[(piece_next + dd) % current_arr]
+        spare = jax.lax.ppermute(
+            local_now, row_axis, [(p, (p + dd) % current_arr) for p in range(current_arr)]
+        )
+        xs_all.append(spare)
+    row_out = jnp.stack(xs_all)[(piece_next - jnp.arange(current_arr)) % current_arr]
+    value_now = find_object(row_out, local_block)
+    return value_now
+
+
+plane_follow = functools.partial(_settle_things, row_axis="row", vector=0, local_block=2)
 
 
 def phase(left_ids, right_ids, modulus, orient):
@@ -204,7 +241,7 @@
         canon = forward_rows(mine)
         mcount = canon.shape[0]
         sent = canon_to_groups(canon, row_count)
-        got = lax.all_to_all(sent, "row", split_axis=0, concat_axis=2, tiled=True)[0]
+        got = plane_follow(sent)[0]
         other = lax.ppermute(got, "wl", perm=[(0, 1), (1, 0)])
         got = got.reshape((2, row_count, own_rows, got.shape[-1]))
         other = other.reshape(got.shape)

time: 724 us -> 910 us (1.26)
  waiting for transfers between devices: 274 us -> 403 us
  starting transfers between devices: 24.9 us -> 80.9 us
    ppermute x0 -> x15, waiting for transfers between devices: none -> 159 us  [_settle_things(): jax.lax.ppermute(local_now, row_axis, [(p, (p + dd) % current_arr) for p...]
    ppermute x0 -> x15, starting transfers between devices: none -> 59.6 us  [_settle_things(): jax.lax.ppermute(local_now, row_axis, [(p, (p + dd) % current_arr) for p...]
    all_to_all x1 -> x0, waiting for transfers between devices: 32.1 us -> none  [local(): lax.all_to_all(sent, 'row', split_axis=0, concat_axis=2, tiled=True)[0]]
    unnamed x118 -> x112, local copies, waits for them, and re-layouts: 48.7 us -> 51.9 us
  transfers between devices with their start and end apart: 9 -> 23, of which waited for: 6 -> 16; matrix products, arithmetic and copies ran while one was open for 36% -> 27% of each run, Pallas kernels for 0% -> 0%
where the time goes in v1:
time: 910 us; the launch traced here: 903 us
  waiting for transfers between devices  403 us (44%)
  matrix products  179 us (20%)
  local copies, waits for them, and re-layouts  166 us (18%)
  starting transfers between devices  80.9 us (9%)
  other arithmetic  69.3 us (8%)
    ppermute x15, waiting for transfers between devices, _settle_things(): jax.lax.ppermute(local_now, row_axis, [(p, (p + dd) % current_arr) for p...  159 us
    all_to_all x1, waiting for transfers between devices, local(): lax.all_to_all(summed, 'row', split_axis=1, concat_axis=1, tiled=True)  91.5 us
    ppermute x1, waiting for transfers between devices, local(): other = lax.ppermute(got, 'wl', perm=[(0, 1), (1, 0)])  82.2 us
    ppermute x15, starting transfers between devices, _settle_things(): jax.lax.ppermute(local_now, row_axis, [(p, (p + dd) % current_arr) for p...  59.6 us
    dot_general x5, matrix products, inverse_cols_half(): jnp.einsum('fken,aenj->fkaj', second_tab, turned, precision=PRECISE)  54.1 us
    unnamed x112, local copies, waits for them, and re-layouts  51.9 us
    ppermute x4, waiting for transfers between devices, local(): incoming.append(lax.ppermute(given, 'wl', perm=[(0, 1), (1, 0)]))  41.1 us
    ppermute x1, waiting for transfers between devices, local(): taken = lax.ppermute(theirs, 'wl', perm=[(0, 1), (1, 0)])  29.8 us
  transfers between devices with their start and end apart: 23, of which 16 were waited for; matrix products, arithmetic and copies ran while one was open for 27% of the time, Pallas kernels for 0%

profile of v1, /device:TPU:10, one launch (start us, length us, event | category | flops | bytes accessed | tf_op | source)
XLA Modules:
  0.0 902.8 jit_solution(2297222661518572096)
XLA Ops:
  46.7 7.7 pad_maximum_fusion
  75.4 14.3 %fusion.17 = f32[2,32,128,2,64,1]{2,4,5,3,1,0:T(8,128)S(1)} fusion(f32[2,32,2,128,128,1]{4,1,3,0,2,5:T(8,128)S(1)} %maximum_bitcast_fusion.1, f32[1,2,2,64,128]{4,3,2,1,0:T(8,128)S(1)} %maximum_bitcast_fusion.22, f32[1,2,2,64,128]{4,3,2,1,0:T(8,128)S(1)} %maximum_bitcast_fusion.21), kind=kOutput, calls=%fused_computation.27 | convolution fusion | flops 3221291008 | bytes 12845056 | tf_op jit(solution)/shard_map/oaern,oenfk->oarfk/dot_general | solution.py:117
  116.3 44.4 %collective-permute-start.5 = (f32[1,2,128,256]{3,2,1,0:T(8,128)S(1)}, f32[1,2,128,256]{3,2,1,0:T(8,128)S(1)}, u32[]{:S(2)}, u32[]{:S(2)}) collective-permute-start(f32[1,2,128,256]{3,2,1,0:T(8,128)S(1)} %get-tuple-element.160), channel_id=1, source_target_pairs={{0,6},{1,7},{2,8},{3,9},{4,10},{5,11},{6,12},{7,13},{8,14},{9,15},... | collective-permute-start | bytes 786440 | tf_op jit(solution)/shard_map/ppermute | solution.py:36
  161.4 94.3 %collective-permute-done.1 = f32[1,2,128,256]{3,2,1,0:T(8,128)S(1)} collective-permute-done((f32[1,2,128,256]{3,2,1,0:T(8,128)S(1)}, f32[1,2,128,256]{3,2,1,0:T(8,128)S(1)}, u32[]{:S(2)}, u32[]{:S(2)}) %collective-permute-start.1) | collective-permute-done | bytes 262176 | tf_op jit(solution)/shard_map/ppermute | solution.py:36
  256.4 16.0 %collective-permute-done.2 = f32[1,2,128,256]{3,2,1,0:T(8,128)S(1)} collective-permute-done((f32[1,2,128,256]{3,2,1,0:T(8,128)S(1)}, f32[1,2,128,256]{3,2,1,0:T(8,128)S(1)}, u32[]{:S(2)}, u32[]{:S(2)}) %collective-permute-start.2) | collective-permute-done | bytes 262176 | tf_op jit(solution)/shard_map/ppermute | solution.py:36
  281.0 8.4 collective-permute-done.4
  293.6 9.8 %collective-permute-done.5 = f32[1,2,128,256]{3,2,1,0:T(8,128)S(1)} collective-permute-done((f32[1,2,128,256]{3,2,1,0:T(8,128)S(1)}, f32[1,2,128,256]{3,2,1,0:T(8,128)S(1)}, u32[]{:S(2)}, u32[]{:S(2)}) %collective-permute-start.5) | collective-permute-done | bytes 262176 | tf_op jit(solution)/shard_map/ppermute | solution.py:36
  321.0 7.2 collective-permute-done.8
  358.2 82.2 %collective-permute-done.15 = f32[2,2048,256]{2,1,0:T(8,128)} collective-permute-done((f32[2,2048,256]{2,1,0:T(8,128)}, f32[2,2048,256]{2,1,0:T(8,128)}, u32[]{:S(2)}, u32[]{:S(2)}) %collective-permute-start.15) | collective-permute-done | bytes 4194336 | tf_op jit(solution)/shard_map/ppermute | solution.py:245
  445.5 10.0 %copy.178 = f32[2,16,2,128,256]{4,2,1,0,3:T(2,128)} copy(f32[2,16,2,128,256]{4,3,0,1,2:T(8,128)S(1)} %pad_maximum_fusion.1) | data formatting | bytes 16777216 | tf_op jit(solution)/shard_map/stack | solution.py:250
  455.5 10.9 %reshape.2242 = f32[2,32,128,256,1,1]{3,1,0,2,4,5:T(8,128)} reshape(f32[2,16,2,128,256]{4,2,1,0,3:T(2,128)} %copy.178) | data formatting | bytes 16777216 | tf_op jit(solution)/shard_map/reshape;reshape | solution.py:131
  466.4 16.7 %fusion.19 = f32[2,32,2,128,256]{4,1,3,2,0:T(8,128)S(1)} fusion(f32[2,32,128,256,1,1]{3,1,0,2,4,5:T(8,128)} %reshape.2242, f32[1,2,2,32,32]{4,3,2,1,0:T(8,128)S(1)} %fusion.98, f32[1,2,2,32,32]{4,3,2,1,0:T(8,128)S(1)} %maximum_bitcast_fusion.31), kind=kOutput, calls=%fused_computation.31 | convolution fusion | flops 3221233664 | bytes 25198592 | tf_op jit(solution)/shard_map/oafeb,ebnj->oafnj/dot_general | solution.py:133
  493.7 25.5 %fusion.22 = f32[2,2,128,32,256]{4,2,3,1,0:T(8,128)S(1)} fusion(f32[2,32,2,128,256,1]{4,1,3,0,2,5:T(8,128)S(1)} %maximum_bitcast_fusion, f32[1,2,2,128,128]{4,3,2,1,0:T(8,128)} %maximum_bitcast_fusion.12, f32[1,2,2,128,128]{4,3,2,1,0:T(8,128)} %maximum_bitcast_fusion.11), kind=kOutput, calls=%fused_computation.32 | convolution fusion | flops 12885032960 | bytes 34078720 | tf_op jit(solution)/shard_map/ofekn,oaenj->ofkaj/dot_general | solution.py:143
  529.3 8.2 copy.184
  554.8 11.5 %copy.168 = bf16[1,2,2,16,256,256]{5,4,3,2,1,0:T(8,128)(2,1)} copy(bf16[1,2,2,16,256,256]{4,5,2,1,3,0:T(8,128)(2,1)} %bitcast.54) | data formatting | bytes 16777216 | tf_op jit(solution)/shard_map/all_to_all | solution.py:259
  566.2 10.8 %fusion.32 = (f32[1,4096,256]{2,1,0:T(8,128)S(1)}, f32[1,4096,256]{2,1,0:T(8,128)S(1)}) fusion(bf16[2,2,4096,256]{3,2,1,0:T(8,128)(2,1)} %bitcast.642, f32[]{:T(128)} %bitcast.157, f32[]{:T(128)} %bitcast.156, f32[2,4096,256]{2,1,0:T(8,128)} %maximum_select_fusion, f32[1,1,128,32,256]{4,3,2,1,0:T(8,128)} %copy.183, f32[]{:T(128)} %bitcast.162, f32[]{:T(128)} %bitcast.161, ...), kind=kLoop, calls=%fused_computation.50 | loop fusion | flops 36700160 | bytes 33554448 | tf_op jit(solution)/shard_map/sub | solution.py:281
  582.0 7.9 fusion.47
  593.1 9.4 %fusion.57 = f32[2,16,32,256]{3,1,2,0:T(8,128)S(1)} fusion(f32[32,2,128,256]{3,0,2,1:T(8,128)S(1)} %pad_maximum_fusion.2, f32[1,2,16,128]{3,2,1,0:T(8,128)S(1)} %copy-done.18, f32[1,2,16,128]{3,2,1,0:T(8,128)S(1)} %copy-done.17), kind=kOutput, calls=%fused_computation.112 | convolution fusion | flops 805314560 | bytes 9469952 | tf_op jit(solution)/shard_map/fken,aenj->fkaj/dot_general | solution.py:162
  604.0 10.5 %fusion.60 = f32[2,16,32,256]{3,1,2,0:T(8,128)} fusion(f32[32,2,128,256]{3,0,2,1:T(8,128)S(1)} %pad_maximum_fusion.2, f32[1,2,16,128]{3,2,1,0:T(8,128)S(1)} %copy-done.16, f32[1,2,16,128]{3,2,1,0:T(8,128)S(1)} %get-tuple-element.195), kind=kOutput, calls=%fused_computation.113 | convolution fusion | flops 805314560 | bytes 9469952 | tf_op jit(solution)/shard_map/fken,aenj->fkaj/dot_general | solution.py:162
  615.1 10.5 %fusion.63 = f32[2,16,32,256]{3,1,2,0:T(8,128)} fusion(f32[32,2,128,256]{3,0,2,1:T(8,128)S(1)} %pad_maximum_fusion.2, f32[1,2,16,128]{3,2,1,0:T(8,128)S(1)} %copy-done.22, f32[1,2,16,128]{3,2,1,0:T(8,128)S(1)} %copy-done.21), kind=kOutput, calls=%fused_computation.114 | convolution fusion | flops 805314560 | bytes 9469952 | tf_op jit(solution)/shard_map/fken,aenj->fkaj/dot_general | solution.py:162
  627.1 10.7 %fusion.66 = f32[2,16,32,256]{3,1,2,0:T(8,128)} fusion(f32[32,2,128,256]{3,0,2,1:T(8,128)S(1)} %pad_maximum_fusion.2, f32[1,2,16,128]{3,2,1,0:T(8,128)S(1)} %copy-done.20, f32[1,2,16,128]{3,2,1,0:T(8,128)S(1)} %copy-done.19), kind=kOutput, calls=%fused_computation.115 | convolution fusion | flops 805314560 | bytes 9469952 | tf_op jit(solution)/shard_map/fken,aenj->fkaj/dot_general | solution.py:162
  638.7 13.0 %fusion.48 = f32[2,64,32,256]{3,1,2,0:T(8,128)S(1)} fusion(f32[32,2,128,256]{3,0,2,1:T(8,128)} %copy-done.2, f32[1,2,64,128]{3,2,1,0:T(8,128)S(1)} %get-tuple-element.180, f32[1,2,64,128]{3,2,1,0:T(8,128)S(1)} %get-tuple-element.179), kind=kOutput, calls=%fused_computation.93 | convolution fusion | flops 3221258240 | bytes 12713984 | tf_op jit(solution)/shard_map/fken,aenj->fkaj/dot_general | solution.py:162
  654.2 19.3 %collective-permute-done.18 = f32[2,16,32,256]{3,1,2,0:T(8,128)} collective-permute-done((f32[2,16,32,256]{3,1,2,0:T(8,128)}, f32[2,16,32,256]{3,1,2,0:T(8,128)}, u32[]{:S(2)}, u32[]{:S(2)}) %collective-permute-start.18) | collective-permute-done | bytes 1048608 | tf_op jit(solution)/shard_map/ppermute | solution.py:297
  673.5 21.8 %collective-permute-done.19 = f32[2,16,32,256]{3,1,2,0:T(8,128)} collective-permute-done((f32[2,16,32,256]{3,1,2,0:T(8,128)}, f32[2,16,32,256]{3,1,2,0:T(8,128)}, u32[]{:S(2)}, u32[]{:S(2)}) %collective-permute-start.19) | collective-permute-done | bytes 1048608 | tf_op jit(solution)/shard_map/ppermute | solution.py:297
  705.6 7.7 all-to-all-start.1
  714.1 91.5 %all-to-all-done.1 = f32[2,16,128,256]{3,2,0,1:T(8,128)} async-done(((f32[2,16,128,256]{3,2,0,1:T(8,128)}), f32[2,16,128,256]{3,2,0,1:T(8,128)}, u32[]{:S(2)}, u32[]{:S(2)}) %all-to-all-start.1) | async-done | bytes 4194336 | tf_op jit(solution)/shard_map/all_to_all | solution.py:306
  805.7 18.1 %convolution_bitcast_fusion = f32[2,32,2,128,256]{4,1,3,2,0:T(8,128)S(1)} fusion(f32[2,16,128,256,1,1]{3,2,0,1,5,4:T(8,128)} %bitcast.213, f32[1,2,2,32,16]{3,4,2,1,0:T(8,128)S(1)} %maximum_bitcast_fusion.45, f32[1,2,2,32,16]{3,4,2,1,0:T(8,128)S(1)} %maximum_bitcast_fusion.44), kind=kOutput, calls=%fused_computation.33 | convolution fusion | flops 1610616832 | bytes 20987904 | tf_op jit(solution)/shard_map/oafem,emRj->oafRj/dot_general | solution.py:184
  829.8 6.9 fusion.38
  836.7 7.1 fusion.51
  847.1 8.1 fusion.40
  855.2 6.9 fusion.52
  863.3 29.8 %collective-permute-done.20 = f32[2,128,2048]{1,2,0:T(8,128)} collective-permute-done((f32[2,128,2048]{1,2,0:T(8,128)S(1)}, f32[2,128,2048]{1,2,0:T(8,128)}, u32[]{:S(2)}, u32[]{:S(2)}) %collective-permute-start.20) | collective-permute-done | bytes 2097184 | tf_op jit(solution)/shard_map/ppermute | solution.py:310
  (275 shorter events, 241.7 us)
Async XLA Ops:
  0.0 348.8 %copy-start = (f32[4,2]{0,1:T(2,128)S(1)}, f32[4,2]{0,1:T(2,128)}, u32[]{:S(2)}) copy-start(f32[4,2]{0,1:T(2,128)} %param.23) | copy-start | bytes 100
  0.0 41.8 %copy-start.23 = (pred[128]{0:T(512)(128)(4,1)}, pred[128]{0:T(512)(128)(4,1)S(1)}, u32[]{:S(2)}) copy-start(pred[128]{0:T(512)(128)(4,1)S(1)} %get-tuple-element.246) | copy-start | bytes 388
  54.4 500.4 %all-to-all-start = ((bf16[16,2,2,256,256]{3,4,2,1,0:T(8,128)(2,1)}), bf16[16,2,2,256,256]{3,4,2,1,0:T(8,128)(2,1)}, u32[]{:S(2)}, u32[]{:S(2)}) async-start(bf16[16,2,2,256,256]{3,4,2,1,0:T(8,128)(2,1)} %pad_maximum_fusion), calls=%async_computation | async-start | bytes 16777216 | tf_op jit(solution)/shard_map/all_to_all | solution.py:259
  108.4 7.9 collective-permute-start
  108.5 147.2 %collective-permute-start.1 = (f32[1,2,128,256]{3,2,1,0:T(8,128)S(1)}, f32[1,2,128,256]{3,2,1,0:T(8,128)S(1)}, u32[]{:S(2)}, u32[]{:S(2)}) collective-permute-start(f32[1,2,128,256]{3,2,1,0:T(8,128)S(1)} %get-tuple-element.164), channel_id=1, source_target_pairs={{0,2},{1,3},{2,4},{3,5},{4,6},{5,7},{6,8},{7,9},{8,10},{9,11},{10,... | collective-permute-start | bytes 786440 | tf_op jit(solution)/shard_map/ppermute | solution.py:36
  110.0 162.4 %collective-permute-start.2 = (f32[1,2,128,256]{3,2,1,0:T(8,128)S(1)}, f32[1,2,128,256]{3,2,1,0:T(8,128)S(1)}, u32[]{:S(2)}, u32[]{:S(2)}) collective-permute-start(f32[1,2,128,256]{3,2,1,0:T(8,128)S(1)} %get-tuple-element.163), channel_id=1, source_target_pairs={{0,3},{1,4},{2,5},{3,6},{4,7},{5,8},{6,9},{7,10},{8,11},{9,12},{10... | collective-permute-start | bytes 786440 | tf_op jit(solution)/shard_map/ppermute | solution.py:36
  112.2 166.0 %collective-permute-start.3 = (f32[1,2,128,256]{3,2,1,0:T(8,128)S(1)}, f32[1,2,128,256]{3,2,1,0:T(8,128)S(1)}, u32[]{:S(2)}, u32[]{:S(2)}) collective-permute-start(f32[1,2,128,256]{3,2,1,0:T(8,128)S(1)} %get-tuple-element.162), channel_id=1, source_target_pairs={{0,4},{1,5},{2,6},{3,7},{4,8},{5,9},{6,10},{7,11},{8,12},{9,13},{1... | collective-permute-start | bytes 786440 | tf_op jit(solution)/shard_map/ppermute | solution.py:36
  112.5 176.9 %collective-permute-start.4 = (f32[1,2,128,256]{3,2,1,0:T(8,128)S(1)}, f32[1,2,128,256]{3,2,1,0:T(8,128)S(1)}, u32[]{:S(2)}, u32[]{:S(2)}) collective-permute-start(f32[1,2,128,256]{3,2,1,0:T(8,128)S(1)} %get-tuple-element.161), channel_id=1, source_target_pairs={{0,5},{1,6},{2,7},{3,8},{4,9},{5,10},{6,11},{7,12},{8,13},{9,14},{... | collective-permute-start | bytes 786440 | tf_op jit(solution)/shard_map/ppermute | solution.py:36
  116.3 187.2 %collective-permute-start.5 = (f32[1,2,128,256]{3,2,1,0:T(8,128)S(1)}, f32[1,2,128,256]{3,2,1,0:T(8,128)S(1)}, u32[]{:S(2)}, u32[]{:S(2)}) collective-permute-start(f32[1,2,128,256]{3,2,1,0:T(8,128)S(1)} %get-tuple-element.160), channel_id=1, source_target_pairs={{0,6},{1,7},{2,8},{3,9},{4,10},{5,11},{6,12},{7,13},{8,14},{9,15},... | collective-permute-start | bytes 786440 | tf_op jit(solution)/shard_map/ppermute | solution.py:36
  255.7 53.3 %collective-permute-start.6 = (f32[1,2,128,256]{3,2,1,0:T(8,128)S(1)}, f32[1,2,128,256]{3,2,1,0:T(8,128)S(1)}, u32[]{:S(2)}, u32[]{:S(2)}) collective-permute-start(f32[1,2,128,256]{3,2,1,0:T(8,128)S(1)} %get-tuple-element.159), channel_id=1, source_target_pairs={{0,7},{1,8},{2,9},{3,10},{4,11},{5,12},{6,13},{7,14},{8,15},{9,0},... | collective-permute-start | bytes 786440 | tf_op jit(solution)/shard_map/ppermute | solution.py:36
  272.4 47.9 %collective-permute-start.7 = (f32[1,2,128,256]{3,2,1,0:T(8,128)S(1)}, f32[1,2,128,256]{3,2,1,0:T(8,128)S(1)}, u32[]{:S(2)}, u32[]{:S(2)}) collective-permute-start(f32[1,2,128,256]{3,2,1,0:T(8,128)S(1)} %get-tuple-element.158), channel_id=1, source_target_pairs={{0,8},{1,9},{2,10},{3,11},{4,12},{5,13},{6,14},{7,15},{8,0},{9,1},... | collective-permute-start | bytes 786440 | tf_op jit(solution)/shard_map/ppermute | solution.py:36
  278.2 50.1 %collective-permute-start.8 = (f32[1,2,128,256]{3,2,1,0:T(8,128)S(1)}, f32[1,2,128,256]{3,2,1,0:T(8,128)S(1)}, u32[]{:S(2)}, u32[]{:S(2)}) collective-permute-start(f32[1,2,128,256]{3,2,1,0:T(8,128)S(1)} %get-tuple-element.157), channel_id=1, source_target_pairs={{0,9},{1,10},{2,11},{3,12},{4,13},{5,14},{6,15},{7,0},{8,1},{9,2},... | collective-permute-start | bytes 786440 | tf_op jit(solution)/shard_map/ppermute | solution.py:36
  289.4 39.6 %collective-permute-start.9 = (f32[1,2,128,256]{3,2,1,0:T(8,128)S(1)}, f32[1,2,128,256]{3,2,1,0:T(8,128)S(1)}, u32[]{:S(2)}, u32[]{:S(2)}) collective-permute-start(f32[1,2,128,256]{3,2,1,0:T(8,128)S(1)} %get-tuple-element.156), channel_id=1, source_target_pairs={{0,10},{1,11},{2,12},{3,13},{4,14},{5,15},{6,0},{7,1},{8,2},{9,3},... | collective-permute-start | bytes 786440 | tf_op jit(solution)/shard_map/ppermute | solution.py:36
  303.4 26.3 %collective-permute-start.10 = (f32[1,2,128,256]{3,2,1,0:T(8,128)S(1)}, f32[1,2,128,256]{3,2,1,0:T(8,128)S(1)}, u32[]{:S(2)}, u32[]{:S(2)}) collective-permute-start(f32[1,2,128,256]{3,2,1,0:T(8,128)S(1)} %get-tuple-element.155), channel_id=1, source_target_pairs={{0,11},{1,12},{2,13},{3,14},{4,15},{5,0},{6,1},{7,2},{8,3},{9,4},{... | collective-permute-start | bytes 786440 | tf_op jit(solution)/shard_map/ppermute | solution.py:36
  309.0 21.5 %collective-permute-start.11 = (f32[1,2,128,256]{3,2,1,0:T(8,128)S(1)}, f32[1,2,128,256]{3,2,1,0:T(8,128)S(1)}, u32[]{:S(2)}, u32[]{:S(2)}) collective-permute-start(f32[1,2,128,256]{3,2,1,0:T(8,128)S(1)} %get-tuple-element.154), channel_id=1, source_target_pairs={{0,12},{1,13},{2,14},{3,15},{4,0},{5,1},{6,2},{7,3},{8,4},{9,5},{1... | collective-permute-start | bytes 786440 | tf_op jit(solution)/shard_map/ppermute | solution.py:36
  320.3 10.9 %collective-permute-start.12 = (f32[1,2,128,256]{3,2,1,0:T(8,128)S(1)}, f32[1,2,128,256]{3,2,1,0:T(8,128)S(1)}, u32[]{:S(2)}, u32[]{:S(2)}) collective-permute-start(f32[1,2,128,256]{3,2,1,0:T(8,128)S(1)} %get-tuple-element.153), channel_id=1, source_target_pairs={{0,13},{1,14},{2,15},{3,0},{4,1},{5,2},{6,3},{7,4},{8,5},{9,6},{10... | collective-permute-start | bytes 786440 | tf_op jit(solution)/shard_map/ppermute | solution.py:36
  328.3 7.3 collective-permute-start.13
  329.0 7.7 collective-permute-start.14
  347.1 93.3 %collective-permute-start.15 = (f32[2,2048,256]{2,1,0:T(8,128)}, f32[2,2048,256]{2,1,0:T(8,128)}, u32[]{:S(2)}, u32[]{:S(2)}) collective-permute-start(f32[2,2048,256]{2,1,0:T(8,128)} %bitcast.141), channel_id=1, source_target_pairs={{0,16},{16,0},{1,17},{17,1},{2,18},{18,2},{3,19},{19,3},{4,20},{20... | collective-permute-start | bytes 12582920 | tf_op jit(solution)/shard_map/ppermute | solution.py:245
  593.0 34.1 %copy-start.2 = (f32[32,2,128,256]{3,0,2,1:T(8,128)}, f32[32,2,128,256]{3,0,2,1:T(8,128)S(1)}, u32[]{:S(2)}) copy-start(f32[32,2,128,256]{3,0,2,1:T(8,128)S(1)} %pad_maximum_fusion.2) | copy-start | bytes 25165828
  593.1 11.0 %copy-start.16 = (f32[1,2,16,128]{3,2,1,0:T(8,128)S(1)}, f32[1,2,16,128]{3,2,1,0:T(8,128)}, u32[]{:S(2)}) copy-start(f32[1,2,16,128]{3,2,1,0:T(8,128)} %get-tuple-element.196) | copy-start | bytes 49156
  602.4 51.8 %collective-permute-start.16 = (f32[2,16,32,256]{3,1,2,0:T(8,128)S(1)}, f32[2,16,32,256]{3,1,2,0:T(8,128)S(1)}, u32[]{:S(2)}, u32[]{:S(2)}) collective-permute-start(f32[2,16,32,256]{3,1,2,0:T(8,128)S(1)} %fusion.57), channel_id=1, source_target_pairs={{0,16},{16,0},{1,17},{17,1},{2,18},{18,2},{3,19},{19,3},{4,20},{20... | collective-permute-start | bytes 3145736 | tf_op jit(solution)/shard_map/ppermute | solution.py:297
  604.0 11.0 %copy-start.21 = (f32[1,2,16,128]{3,2,1,0:T(8,128)S(1)}, f32[1,2,16,128]{3,2,1,0:T(8,128)}, u32[]{:S(2)}) copy-start(f32[1,2,16,128]{3,2,1,0:T(8,128)} %get-tuple-element.197) | copy-start | bytes 49156
  604.0 11.0 %copy-start.22 = (f32[1,2,16,128]{3,2,1,0:T(8,128)S(1)}, f32[1,2,16,128]{3,2,1,0:T(8,128)}, u32[]{:S(2)}) copy-start(f32[1,2,16,128]{3,2,1,0:T(8,128)} %get-tuple-element.198) | copy-start | bytes 49156
  614.5 39.7 %collective-permute-start.17 = (f32[2,16,32,256]{3,1,2,0:T(8,128)}, f32[2,16,32,256]{3,1,2,0:T(8,128)S(1)}, u32[]{:S(2)}, u32[]{:S(2)}) collective-permute-start(f32[2,16,32,256]{3,1,2,0:T(8,128)} %fusion.60), channel_id=1, source_target_pairs={{0,16},{16,0},{1,17},{17,1},{2,18},{18,2},{3,19},{19,3},{4,20},{20... | collective-permute-start | bytes 3145736 | tf_op jit(solution)/shard_map/ppermute | solution.py:297
  615.1 12.0 %copy-start.19 = (f32[1,2,16,128]{3,2,1,0:T(8,128)S(1)}, f32[1,2,16,128]{3,2,1,0:T(8,128)}, u32[]{:S(2)}) copy-start(f32[1,2,16,128]{3,2,1,0:T(8,128)} %get-tuple-element.199) | copy-start | bytes 49156
  615.1 12.0 %copy-start.20 = (f32[1,2,16,128]{3,2,1,0:T(8,128)S(1)}, f32[1,2,16,128]{3,2,1,0:T(8,128)}, u32[]{:S(2)}) copy-start(f32[1,2,16,128]{3,2,1,0:T(8,128)} %get-tuple-element.200) | copy-start | bytes 49156
  625.6 48.0 %collective-permute-start.18 = (f32[2,16,32,256]{3,1,2,0:T(8,128)}, f32[2,16,32,256]{3,1,2,0:T(8,128)}, u32[]{:S(2)}, u32[]{:S(2)}) collective-permute-start(f32[2,16,32,256]{3,1,2,0:T(8,128)} %fusion.63), channel_id=1, source_target_pairs={{0,16},{16,0},{1,17},{17,1},{2,18},{18,2},{3,19},{19,3},{4,20},{20... | collective-permute-start | bytes 3145736 | tf_op jit(solution)/shard_map/ppermute | solution.py:297
  637.8 57.6 %collective-permute-start.19 = (f32[2,16,32,256]{3,1,2,0:T(8,128)}, f32[2,16,32,256]{3,1,2,0:T(8,128)}, u32[]{:S(2)}, u32[]{:S(2)}) collective-permute-start(f32[2,16,32,256]{3,1,2,0:T(8,128)} %fusion.66), channel_id=1, source_target_pairs={{0,16},{16,0},{1,17},{17,1},{2,18},{18,2},{3,19},{19,3},{4,20},{20... | collective-permute-start | bytes 3145736 | tf_op jit(solution)/shard_map/ppermute | solution.py:297
  705.6 100.1 %all-to-all-start.1 = ((f32[2,16,128,256]{3,2,0,1:T(8,128)}), f32[2,16,128,256]{3,2,0,1:T(8,128)}, u32[]{:S(2)}, u32[]{:S(2)}) async-start(f32[2,16,128,256]{3,2,0,1:T(8,128)} %copy.197), calls=%async_computation.1 | async-start | bytes 8388608 | tf_op jit(solution)/shard_map/all_to_all | solution.py:306
  829.8 14.0 %copy-start.6 = (f32[32,2,128,128,1]{3,0,2,1,4:T(8,128)}, f32[32,2,128,128,1]{3,0,2,1,4:T(8,128)S(1)}, u32[]{:S(2)}) copy-start(f32[32,2,128,128,1]{3,0,2,1,4:T(8,128)S(1)} %maximum_bitcast_fusion.5) | copy-start | bytes 12582916
  845.0 48.0 %collective-permute-start.20 = (f32[2,128,2048]{1,2,0:T(8,128)S(1)}, f32[2,128,2048]{1,2,0:T(8,128)}, u32[]{:S(2)}, u32[]{:S(2)}) collective-permute-start(f32[2,128,2048]{1,2,0:T(8,128)S(1)} %bitcast.651), channel_id=1, source_target_pairs={{0,16},{16,0},{1,17},{17,1},{2,18},{18,2},{3,19},{19,3},{4,20},{20... | collective-permute-start | bytes 6291464 | tf_op jit(solution)/shard_map/ppermute | solution.py:310
  (17 other events, 84.0 us)
